TPU v7x, 256 devices: a whole 4x4x8 slice. The times are simulated.
256 devices in a mesh: ctx: 64 (over y, z, core), ch: 4 (over x).
Axes of the slice: x: 4, y: 4, z: 8, core: 2. Of those that a mesh axis runs over, the one named last changes fastest.
Arguments:
- tokens: bfloat16 [16384, 4096], P('ctx', 'ch'), may hold values from -6 to 6
- in_weight: bfloat16 [3, 4096, 4096], P(None, 'ctx', 'ch'), may hold values from -0.09375 to 0.09375
- short_taps: float32 [3, 3, 4096], P(None, None, 'ch'), may hold values from -4 to 4
- long_filter: float32 [4, 1024, 16384], P('ch', 'ctx'), may hold values from -0.046875 to 0.046875
- skip_gain: float32 [4, 1024], P('ch', 'ctx'), may hold values from 0.25 to 2
Outputs:
- gated_output: bfloat16 [4096, 16384], P('ch', 'ctx')
All inputs are finite; a program needn't handle non-finite values.
Results may differ from a plain program's by a relative error of at most 0.015.
Values may be sent and summed in bfloat16 or wider, within the bound.
No kernel may reach another device: no remote copies, remote signals or barrier semaphores. Data moves between devices by JAX's collectives and lax.ppermute only.
A program may use at most 128 MiB of HBM per device.

v0:
```python
import math
import jax
import jax.numpy as jnp
from jax import lax
import numpy as np
from jax.sharding import Mesh, NamedSharding
from jax.sharding import PartitionSpec as P

BLOCK = 1024
FACTOR = 32


def shifted(block, axis, size, distance):
    route = [(i - distance, i) for i in range(size) if 0 <= i - distance < size]
    return lax.ppermute(block, axis, route)


def unit_wave(rows, cols, period, scale_rows):
    outer = rows // FACTOR
    hi = jnp.arange(outer, dtype=jnp.int32)[:, None] * (FACTOR * scale_rows)
    lo = jnp.arange(FACTOR, dtype=jnp.int32)[:, None] * scale_rows
    col = jnp.arange(cols, dtype=jnp.int32)[None, :]
    step = 2.0 * math.pi / period
    hi_phase = step * (hi * col % period).astype(jnp.float32)
    lo_phase = step * (lo * col % period).astype(jnp.float32)
    hc, hs = (jnp.cos(hi_phase)[:, None, :], jnp.sin(hi_phase)[:, None, :])
    lc, ls = (jnp.cos(lo_phase)[None, :, :], jnp.sin(lo_phase)[None, :, :])
    cos_t = (hc * lc - hs * ls).reshape(rows, cols)
    sin_t = (hs * lc + hc * ls).reshape(rows, cols)
    return (cos_t, sin_t)


def spectral_tables(tile_extent):
    period = 2 * tile_extent
    cos_f, sin_f = unit_wave(tile_extent, tile_extent, period, 1)
    alternating = jnp.where(jnp.arange(tile_extent) % 2 == 0, 1.0, -1.0).astype(jnp.float32)
    first_col = (jnp.arange(tile_extent) == 0)[None, :]
    forward = jnp.concatenate(
        [cos_f, jnp.where(first_col, alternating[:, None], -sin_f)], axis=1
    ).astype(jnp.bfloat16)
    cos_b, sin_b = unit_wave(tile_extent, period, period, 1)
    first_row = (jnp.arange(tile_extent) == 0)[:, None]
    alt_t = jnp.where(jnp.arange(period) % 2 == 0, 1.0, -1.0).astype(jnp.float32)[None, :]
    weights = jnp.where(first_row, 1.0, 2.0) / period
    inverse = jnp.concatenate(
        [weights * cos_b, jnp.where(first_row, alt_t / period, -(2.0 / period) * sin_b)], axis=0
    ).astype(jnp.bfloat16)
    return (forward, inverse)


def filter_spectra(kernel_table_lines, forward, tile_extent):
    lane_total, context_extent = kernel_table_lines.shape
    groups = context_extent // tile_extent
    kernel = (
        kernel_table_lines.astype(jnp.bfloat16)
        .reshape(lane_total, groups, tile_extent)
        .transpose(1, 0, 2)
        .reshape(groups * lane_total, tile_extent)
    )
    spec_k = jnp.dot(kernel, forward, preferred_element_type=jnp.float32)
    return spec_k.reshape(groups, lane_total, 2 * tile_extent)


def global_causal_smear(gate_wave, spec_k, leftover_lines, forward, inverse, tile_extent):
    lane_total, context_extent = gate_wave.shape
    groups = context_extent // tile_extent
    slot0 = (jnp.arange(tile_extent) == 0)[None, None, :]
    source = gate_wave.reshape(lane_total * groups, tile_extent)
    spec_x = jnp.dot(source, forward, preferred_element_type=jnp.float32)
    spec_x = spec_x.reshape(lane_total, groups, 2 * tile_extent)
    x_re, x_im = (spec_x[:, :, :tile_extent], spec_x[:, :, tile_extent:])
    k_re, k_im = (spec_k[:, :, :tile_extent], spec_k[:, :, tile_extent:])
    pad = jnp.zeros((lane_total, groups - 1, tile_extent), jnp.float32)
    xp_re = jnp.concatenate([pad, x_re], axis=1)
    xp_im = jnp.concatenate([pad, x_im], axis=1)
    rr = ii = ri = ir = None
    for offset in range(groups):
        s_re = xp_re[:, groups - 1 - offset : 2 * groups - 1 - offset]
        s_im = xp_im[:, groups - 1 - offset : 2 * groups - 1 - offset]
        f_re = k_re[offset][:, None, :]
        f_im = k_im[offset][:, None, :]
        terms = (f_re * s_re, f_im * s_im, f_re * s_im, f_im * s_re)
        if rr is None:
            rr, ii, ri, ir = terms
        else:
            rr, ii, ri, ir = (rr + terms[0], ii + terms[1], ri + terms[2], ir + terms[3])
    y_re = rr - jnp.where(slot0, 0.0, ii)
    y_im = jnp.where(slot0, ii, ri + ir)
    packed = jnp.concatenate([y_re, y_im], axis=2).astype(jnp.bfloat16)
    rows = jnp.dot(
        packed.reshape(lane_total * groups, 2 * tile_extent),
        inverse,
        preferred_element_type=jnp.float32,
    ).reshape(lane_total, groups, 2 * tile_extent)
    front_half = rows[:, :, :tile_extent]
    back_half = rows[:, :, tile_extent:]
    carried = jnp.concatenate(
        [jnp.zeros((lane_total, 1, tile_extent), jnp.float32), back_half[:, :-1]], axis=1
    )
    affine_mapping = (front_half + carried).reshape(lane_total, context_extent)
    wide = gate_wave.astype(jnp.float32)
    return (affine_mapping + leftover_lines[:, None] * wide).astype(jnp.bfloat16)


def short_conv(projected_float, local_taps, previous):
    context_extent = projected_float.shape[2]
    extended = jnp.concatenate([previous, projected_float], axis=2)
    result = jnp.zeros_like(projected_float)
    for offset in range(3):
        result = (
            result
            + local_taps[:, offset, :][:, :, None]
            * extended[:, :, 2 - offset : 2 - offset + context_extent]
        )
    return result


def make_shards(n_ctx, n_ch, tile_extent):
    ctx = ("yh", "cq")
    swap = [(0, 1), (1, 0)]

    def featured(projected, taps):
        local_tokens = projected.shape[2]
        previous = shifted(projected[:, :, local_tokens - 2 :], ctx, n_ctx, 1)
        return short_conv(projected.astype(jnp.float32), taps, previous.astype(jnp.float32))

    def by_half(half, own, other):
        first = jnp.where(half == 0, own, other)
        second = jnp.where(half == 0, other, own)
        return jnp.stack([first, second])

    def shards(tokens, in_weight, short_taps, long_filter, skip_gain):
        half = lax.axis_index("yh")
        local_tokens, local_features = tokens.shape
        branches, local_rows, lanes = in_weight.shape
        width = lanes // 2
        n_q = n_ctx // 2
        own_cols = lax.dynamic_slice_in_dim(in_weight, half * width, width, axis=2)
        other_cols = lax.dynamic_slice_in_dim(in_weight, (1 - half) * width, width, axis=2)
        partner_rows = lax.ppermute(other_cols, "yh", swap)
        rows_pair = jnp.stack(list(by_half(half, own_cols, partner_rows)), axis=1)
        gathered = lax.all_gather(rows_pair, "cq", axis=2, tiled=False)
        whole_weight = gathered.reshape(branches, -1, width)
        partner_tokens = lax.ppermute(tokens, "yh", swap)
        token_pair = by_half(half, tokens, partner_tokens)
        copies = jnp.broadcast_to(token_pair[None], (n_ch,) + token_pair.shape)
        pieces = lax.all_to_all(copies, "ch", split_axis=0, concat_axis=3, tiled=True)
        whole_tokens = pieces.reshape(2 * local_tokens, n_ch * local_features)
        forward, inverse = spectral_tables(tile_extent)
        spec_k = filter_spectra(long_filter[0], forward, tile_extent)
        whole_weight, forward, inverse, spec_k = lax.optimization_barrier(
            (whole_weight, forward, inverse, spec_k)
        )
        summed = jnp.einsum(
            "pdc,ld->pcl", whole_weight, whole_tokens, preferred_element_type=jnp.float32
        ).astype(jnp.bfloat16)
        own_part = lax.dynamic_slice_in_dim(summed[0:1], half * local_tokens, local_tokens, axis=2)
        other_part = lax.dynamic_slice_in_dim(
            summed[0:1], (1 - half) * local_tokens, local_tokens, axis=2
        )
        received = lax.ppermute(other_part, "yh", swap)
        q = lax.axis_index("cq")
        blocks = summed[1:3].reshape(2, width, 2, local_tokens)
        tails = blocks[:, :, :, local_tokens - 2 :].transpose(0, 2, 3, 1).reshape(-1, width)
        ring = [(i, (i + 1) % n_q) for i in range(n_q)]
        arrived = lax.ppermute(tails, "cq", ring).reshape(2, 2, 2, width).transpose(0, 3, 1, 2)
        first = jnp.concatenate([jnp.zeros_like(arrived[:, :, :1]), arrived[:, :, :1]], axis=2)
        halo = jnp.where(q == 0, first, arrived)
        taps12 = lax.dynamic_slice_in_dim(short_taps[1:3], half * width, width, axis=2)
        extended = jnp.concatenate([halo, blocks], axis=3).astype(jnp.float32)
        embed12 = None
        for offset in range(3):
            term = (
                taps12[:, offset, :][:, :, None, None]
                * extended[:, :, :, 2 - offset : 2 - offset + local_tokens]
            )
            embed12 = term if embed12 is None else embed12 + term
        gate_wave = (embed12[0] * embed12[1]).astype(jnp.bfloat16)
        lanes_each = width // n_q
        outgoing12 = gate_wave.reshape(n_q, lanes_each, 2, local_tokens)
        got = lax.all_to_all(outgoing12, "cq", split_axis=0, concat_axis=0, tiled=True)
        received, got = lax.optimization_barrier((received, got))
        per_channel_view = got.transpose(1, 2, 0, 3).reshape(lanes_each, -1)
        projected0 = jnp.concatenate(list(by_half(half, own_part, received)), axis=1)
        embed0 = featured(projected0, short_taps[0:1])
        blended_lines = global_causal_smear(
            per_channel_view, spec_k, skip_gain[0], forward, inverse, tile_extent
        )
        lines, span = blended_lines.shape
        outgoing = blended_lines.reshape(lines, n_ctx, span // n_ctx).transpose(1, 0, 2)
        returned = lax.all_to_all(outgoing, ctx, split_axis=0, concat_axis=0, tiled=True)
        by_token = returned.reshape(n_ctx * lines, span // n_ctx)
        gated_output = (embed0[0] * by_token.astype(jnp.float32)).astype(jnp.bfloat16)
        return gated_output

    return shards


def solution(mesh):
    n_ctx = mesh.shape["ctx"]
    grid = np.asarray(mesh.devices).reshape(2, n_ctx // 2, mesh.shape["ch"])
    split_mesh = Mesh(grid, ("yh", "cq", "ch"))
    ctx = ("yh", "cq")
    placed = (
        P(ctx, "ch"),
        P(None, ctx, "ch"),
        P(None, None, "ch"),
        P("ch", ctx, None),
        P("ch", ctx),
    )
    mapped = jax.shard_map(
        make_shards(n_ctx, mesh.shape["ch"], BLOCK),
        mesh=split_mesh,
        in_specs=placed,
        out_specs=P("ch", ctx),
        check_vma=False,
    )
    out_sharding = NamedSharding(mesh, P("ch", "ctx"))

    def run(*args):
        return lax.with_sharding_constraint(mapped(*args), out_sharding)

    return run
```

profile of v0, /device:TPU:1, one launch (start us, length us, event | category | flops | bytes accessed | tf_op | source)
XLA Modules:
  0.0 207.8 jit_solution(14225138241267218314)
XLA Ops:
  6.5 1.0 constant_dynamic-slice_fusion.4
  7.5 3.8 %collective-permute-start = (bf16[3,64,512]{2,1,0:T(8,128)(2,1)S(1)}, bf16[3,64,512]{2,1,0:T(8,128)(2,1)S(1)}, u32[]{:S(2)}, u32[]{:S(2)}) collective-permute-start(bf16[3,64,512]{2,1,0:T(8,128)(2,1)S(1)} %constant_dynamic-slice_fusion.4), channel_id=1, source_target_pairs={{0,128},{128,0},{1,129},{129,1},{2,130},{130,2},{3,131},{131,3},{4... | collective-permute-start | bytes 589832 | tf_op jit(solution)/shard_map/ppermute | solution.py:140
  11.3 3.6 %collective-permute-done = bf16[3,64,512]{2,1,0:T(8,128)(2,1)S(1)} collective-permute-done((bf16[3,64,512]{2,1,0:T(8,128)(2,1)S(1)}, bf16[3,64,512]{2,1,0:T(8,128)(2,1)S(1)}, u32[]{:S(2)}, u32[]{:S(2)}) %collective-permute-start) | collective-permute-done | bytes 196640 | tf_op jit(solution)/shard_map/ppermute | solution.py:140
  14.9 1.0 select_bitcast_fusion.3
  15.9 0.8 pad_maximum_fusion.5
  16.7 3.8 %collective-permute-start.1 = (bf16[256,1024]{1,0:T(8,128)(2,1)}, bf16[256,1024]{1,0:T(8,128)(2,1)}, u32[]{:S(2)}, u32[]{:S(2)}) collective-permute-start(bf16[256,1024]{1,0:T(8,128)(2,1)} %param.5), channel_id=1, source_target_pairs={{0,128},{128,0},{1,129},{129,1},{2,130},{130,2},{3,131},{131,3},{4... | collective-permute-start | bytes 1572872 | tf_op jit(solution)/shard_map/ppermute | solution.py:144
  20.5 1.3 convert_element_type.115
  22.1 1.1 copy.24
  24.4 1.0 fusion.42
  26.3 0.8 subtract_convert_fusion
  27.4 2.6 %pad_maximum_fusion.1 = bf16[1024,2048]{1,0:T(8,128)(2,1)} fusion(bf16[1024,1024]{1,0:T(8,128)(2,1)S(1)} %fusion.6, bf16[1024,1024]{1,0:T(8,128)(2,1)S(1)} %bitcast.149), kind=kLoop, calls=%fused_computation.39 | loop fusion | flops 8388608 | bytes 8388608 | tf_op jit(solution)/shard_map/concatenate | solution.py:38
  30.0 1.1 fusion.45
  31.1 3.5 %add_multiply_fusion = bf16[32,32,2048]{2,1,0:T(8,128)(2,1)} fusion(f32[32,2048]{1,0:T(8,128)S(1)} %get-tuple-element.69, f32[32,2048]{1,0:T(8,128)S(1)} %get-tuple-element.64, f32[32,2048]{1,0:T(8,128)S(1)} %get-tuple-element.70, f32[32,2048]{1,0:T(8,128)S(1)} %get-tuple-element.63), kind=kLoop, calls=%fused_computation.7 | loop fusion | flops 10485760 | bytes 5242880 | tf_op jit(solution)/shard_map/mul | solution.py:46
  34.7 1.1 select_bitcast_fusion.1
  35.9 2.5 %broadcast_in_dim.111 = bf16[4,2,256,1024]{3,2,1,0:T(8,128)(2,1)} broadcast(bf16[2,256,1024]{2,1,0:T(8,128)(2,1)S(1)} %pad_maximum_fusion.3), dimensions={1,2,3} | broadcast | bytes 5242880 | tf_op jit(solution)/shard_map/broadcast_in_dim | solution.py:146
  38.4 5.1 %all-to-all-start = ((bf16[4,2,256,1024]{3,2,1,0:T(8,128)(2,1)}), bf16[4,2,256,1024]{3,2,1,0:T(8,128)(2,1)}, u32[]{:S(2)}, u32[]{:S(2)}) async-start(bf16[4,2,256,1024]{3,2,1,0:T(8,128)(2,1)} %broadcast_in_dim.111), calls=%async_computation | async-start | bytes 8388608 | tf_op jit(solution)/shard_map/all_to_all | solution.py:147
  43.5 4.5 %fusion.67 = f32[2048,256]{0,1:T(8,128)} fusion(bf16[256,1024]{1,0:T(8,128)(2,1)} %bitcast.159, bf16[1024,1024]{1,0:T(8,128)(2,1)} %copy-done.1, bf16[1024,1024]{1,0:T(8,128)(2,1)S(1)} %bitcast.150), kind=kOutput, calls=%fused_computation.195 | convolution fusion | flops 1082130432 | bytes 6815744 | tf_op jit(solution)/shard_map/dot_general | solution.py:60
  48.0 2.9 %fusion.2 = bf16[1024,2048]{1,0:T(8,128)(2,1)} fusion(bf16[32,32,2048]{2,1,0:T(8,128)(2,1)S(1)} %copy-done, bf16[2048]{0:T(1024)(128)(2,1)S(1)} %select_multiply_fusion, pred[1024]{0:T(1024)(128)(4,1)S(1)} %iota_compare_fusion), kind=kLoop, calls=%fused_computation.4 | loop fusion | flops 2097152 | bytes 8393728 | tf_op jit(solution)/shard_map/convert.5 | solution.py:221
  50.9 1.2 multiply_subtract_fusion
  52.1 2.5 %fusion.3 = bf16[1024,2048]{1,0:T(8,128)(2,1)} fusion(f32[32,32,2048]{2,1,0:T(8,128)S(1)} %multiply_subtract_fusion, f32[1024]{0:T(1024)S(1)} %select_multiply_fusion.1), kind=kLoop, calls=%fused_computation.6 | loop fusion | flops 4194304 | bytes 12587008 | tf_op jit(solution)/shard_map/convert.4 | solution.py:221
  54.6 8.5 %pad_maximum_fusion = bf16[2048,2048]{1,0:T(8,128)(2,1)} fusion(bf16[1024,2048]{1,0:T(8,128)(2,1)} %fusion.2, bf16[1024,2048]{1,0:T(8,128)(2,1)} %fusion.3), kind=kLoop, calls=%fused_computation | loop fusion | flops 16777216 | bytes 16777216 | tf_op jit(solution)/shard_map/concatenate | solution.py:45
  63.1 27.3 %all-to-all-done = bf16[4,2,256,1024]{3,2,1,0:T(8,128)(2,1)} async-done(((bf16[4,2,256,1024]{3,2,1,0:T(8,128)(2,1)}), bf16[4,2,256,1024]{3,2,1,0:T(8,128)(2,1)}, u32[]{:S(2)}, u32[]{:S(2)}) %all-to-all-start) | async-done | bytes 4194336 | tf_op jit(solution)/shard_map/all_to_all | solution.py:147
  90.4 7.4 %copy.25 = bf16[1,2,256,4,1024]{4,3,2,1,0:T(4,128)(2,1)} copy(bf16[1,2,256,4,1024]{4,2,1,3,0:T(8,128)(2,1)} %bitcast.16) | data formatting | bytes 8388608 | tf_op jit(solution)/shard_map/all_to_all | solution.py:147
  97.8 7.8 %reshape.442 = bf16[512,4096,1]{1,0,2:T(8,128)(2,1)} reshape(bf16[1,2,256,4,1024]{4,3,2,1,0:T(4,128)(2,1)} %copy.25) | data formatting | bytes 8388608 | tf_op jit(solution)/shard_map/reshape | solution.py:148
  105.7 10.9 %convolution_convert_fusion = bf16[3,512,512]{1,2,0:T(8,128)(2,1)S(1)} fusion(bf16[512,4096,1]{1,0,2:T(8,128)(2,1)} %reshape.442, bf16[3,4096,512]{2,1,0:T(8,128)(2,1)} %bitcast.166), kind=kOutput, calls=%fused_computation.51 | convolution fusion | flops 6443237376 | bytes 18350080 | tf_op jit(solution)/shard_map/pdc,ld->pcl/dot_general | solution.py:154
  116.6 1.2 copy-done.5
  117.8 4.5 %collective-permute-start.3 = (bf16[8,512]{1,0:T(8,128)(2,1)S(1)}, bf16[8,512]{1,0:T(8,128)(2,1)S(1)}, u32[]{:S(2)}, u32[]{:S(2)}) collective-permute-start(bf16[8,512]{1,0:T(8,128)(2,1)S(1)} %reshape.435), channel_id=1, source_target_pairs={{0,4},{4,8},{8,12},{12,16},{16,20},{20,24},{24,28},{28,32},{32,36}... | collective-permute-start | bytes 24584 | tf_op jit(solution)/shard_map/ppermute | solution.py:166
  124.2 1.7 fusion.7
  126.0 0.9 copy.28
  126.8 10.7 %all-to-all-start.1 = ((bf16[32,16,2,256]{3,1,2,0:T(8,128)(2,1)}), bf16[32,16,2,256]{3,1,2,0:T(8,128)(2,1)S(1)}, u32[]{:S(2)}, u32[]{:S(2)}) async-start(bf16[32,16,2,256]{3,1,2,0:T(8,128)(2,1)} %copy.28), calls=%async_computation.1 | async-start | bytes 1048576 | tf_op jit(solution)/shard_map/all_to_all | solution.py:181
  137.6 1.1 slice.381
  138.6 0.8 copy-done.2
  139.5 1.6 collective-permute-start.2
  141.1 0.9 slice_bitcast_fusion.30
  142.0 0.8 slice_bitcast_fusion.31
  142.8 9.8 %collective-permute-done.2 = bf16[1,512,256]{1,2,0:T(8,128)(2,1)} collective-permute-done((bf16[1,512,256]{1,2,0:T(8,128)(2,1)S(1)}, bf16[1,512,256]{1,2,0:T(8,128)(2,1)}, u32[]{:S(2)}, u32[]{:S(2)}) %collective-permute-start.2) | collective-permute-done | bytes 262176 | tf_op jit(solution)/shard_map/ppermute | solution.py:161
  152.6 1.5 all-to-all-done.1
  154.9 3.6 %fusion.4 = f32[16,16,2048]{2,1,0:T(8,128)S(1)} fusion(bf16[16,16,1024]{2,1,0:T(8,128)(2,1)S(1)} %dot_general.19, bf16[1024,2048]{1,0:T(8,128)(2,1)} %pad_maximum_fusion.1), kind=kOutput, calls=%fused_computation.40 | convolution fusion | flops 1073741824 | bytes 6815744 | tf_op jit(solution)/shard_map/dot_general | solution.py:69
  159.0 4.5 %subtract_convert_fusion.1 = bf16[16,16,1024]{2,1,0:T(8,128)(2,1)S(1)} fusion(f32[16,16,1024]{2,1,0:T(8,128)S(1)} %get-tuple-element.50, f32[16,1024]{1,0:T(8,128)S(1)} %copy-done.9, f32[16,1024]{1,0:T(8,128)S(1)} %copy-done.10, f32[16,1024]{1,0:T(8,128)S(1)} %copy-done.12, f32[16,1024]{1,0:T(8,128)S(1)} %copy-done.13, f32[16,1024]{1,0:T(8,128)S(1)} %copy-done.14, ...), kind=kLoop, calls=%fused_computation.75 | loop fusion | flops 17039360 | bytes 4719616 | tf_op jit(solution)/shard_map/convert.2 | solution.py:221
  163.6 5.2 %select_convert_fusion = bf16[16,16,1024]{2,1,0:T(8,128)(2,1)S(1)} fusion(f32[16,16,1024]{2,1,0:T(8,128)S(1)} %get-tuple-element.50, f32[16,16,1024]{2,1,0:T(8,128)S(1)} %get-tuple-element.49, f32[16,1024]{1,0:T(8,128)S(1)} %get-tuple-element.18, f32[16,1024]{1,0:T(8,128)S(1)} %get-tuple-element.19, f32[16,1024]{1,0:T(8,128)S(1)} %get-tuple-element.20, ...), kind=kLoop, calls=%fused_computation.74 | loop fusion | flops 25165824 | bytes 4719616 | tf_op jit(solution)/shard_map/convert.3 | solution.py:221
  168.9 2.4 %fusion = f32[16,16,2048]{2,1,0:T(8,128)S(1)} fusion(bf16[2048,2048]{1,0:T(8,128)(2,1)S(1)} %bitcast.148, bf16[16,16,1024]{2,1,0:T(8,128)(2,1)S(1)} %select_convert_fusion, bf16[16,16,1024]{2,1,0:T(8,128)(2,1)S(1)} %subtract_convert_fusion.1), kind=kOutput, calls=%fused_computation.1 | convolution fusion | flops 2149580800 | bytes 11534336 | tf_op jit(solution)/shard_map/dot_general | solution.py:90
  172.1 1.4 fusion.22
  173.5 8.1 %all-to-all-start.2 = ((bf16[64,16,256]{2,1,0:T(8,128)(2,1)}), bf16[64,16,256]{2,1,0:T(8,128)(2,1)S(1)}, u32[]{:S(2)}, u32[]{:S(2)}) async-start(bf16[64,16,256]{2,1,0:T(8,128)(2,1)} %bitcast.61), calls=%async_computation.2 | async-start | bytes 1048576 | tf_op jit(solution)/shard_map/all_to_all | solution.py:191
  181.6 1.0 broadcast_select_fusion
  182.7 3.5 %collective-permute-start.4 = (bf16[1,1024,2]{1,2,0:T(2,128)(2,1)S(1)}, bf16[1,1024,2]{1,2,0:T(2,128)(2,1)S(1)}, u32[]{:S(2)}, u32[]{:S(2)}) collective-permute-start(bf16[1,1024,2]{1,2,0:T(2,128)(2,1)S(1)} %fusion.60), channel_id=1, source_target_pairs={{0,4},{4,8},{8,12},{12,16},{16,20},{20,24},{24,28},{28,32},{32,36}... | collective-permute-start | bytes 12296 | tf_op jit(solution)/shard_map/ppermute | solution.py:15
  186.4 3.7 %collective-permute-done.4 = bf16[1,1024,2]{1,2,0:T(2,128)(2,1)S(1)} collective-permute-done((bf16[1,1024,2]{1,2,0:T(2,128)(2,1)S(1)}, bf16[1,1024,2]{1,2,0:T(2,128)(2,1)S(1)}, u32[]{:S(2)}, u32[]{:S(2)}) %collective-permute-start.4) | collective-permute-done | bytes 4128 | tf_op jit(solution)/shard_map/ppermute | solution.py:15
  190.1 9.0 %all-to-all-done.2 = bf16[64,16,256]{2,1,0:T(8,128)(2,1)S(1)} async-done(((bf16[64,16,256]{2,1,0:T(8,128)(2,1)}), bf16[64,16,256]{2,1,0:T(8,128)(2,1)S(1)}, u32[]{:S(2)}, u32[]{:S(2)}) %all-to-all-start.2) | async-done | bytes 524320 | tf_op jit(solution)/shard_map/all_to_all | solution.py:191
  199.9 1.0 copy.33
  (104 shorter events, 7.5 us)
Async XLA Ops:
  6.5 16.7 %slice-start.2 = ((f32[3,3,1024]{2,1,0:T(4,128)}), f32[2,3,1024]{2,1,0:T(4,128)S(1)}, s32[]{:S(2)}) async-start(f32[3,3,1024]{2,1,0:T(4,128)} %param.7), calls=%async_computation.6 | async-start | bytes 65536 | tf_op jit(solution)/shard_map/slice | solution.py:169
  6.5 99.1 %all-gather.3.cloned.1.call-start = ((), (), s32[]{:S(2)}) async-start(), calls=%async_computation.3 | async-start | bytes 12976128 | tf_op jit(solution)/shard_map/all_gather | solution.py:142
  7.5 7.4 %collective-permute-start = (bf16[3,64,512]{2,1,0:T(8,128)(2,1)S(1)}, bf16[3,64,512]{2,1,0:T(8,128)(2,1)S(1)}, u32[]{:S(2)}, u32[]{:S(2)}) collective-permute-start(bf16[3,64,512]{2,1,0:T(8,128)(2,1)S(1)} %constant_dynamic-slice_fusion.4), channel_id=1, source_target_pairs={{0,128},{128,0},{1,129},{129,1},{2,130},{130,2},{3,131},{131,3},{4... | collective-permute-start | bytes 589832 | tf_op jit(solution)/shard_map/ppermute | solution.py:140
  16.7 18.0 %collective-permute-start.1 = (bf16[256,1024]{1,0:T(8,128)(2,1)}, bf16[256,1024]{1,0:T(8,128)(2,1)}, u32[]{:S(2)}, u32[]{:S(2)}) collective-permute-start(bf16[256,1024]{1,0:T(8,128)(2,1)} %param.5), channel_id=1, source_target_pairs={{0,128},{128,0},{1,129},{129,1},{2,130},{130,2},{3,131},{131,3},{4... | collective-permute-start | bytes 1572872 | tf_op jit(solution)/shard_map/ppermute | solution.py:144
  27.4 2.6 %copy-start.1 = (bf16[1024,1024]{1,0:T(8,128)(2,1)}, bf16[1024,1024]{1,0:T(8,128)(2,1)S(1)}, u32[]{:S(2)}) copy-start(bf16[1024,1024]{1,0:T(8,128)(2,1)S(1)} %fusion.6) | copy-start | bytes 6291460
  30.0 4.6 %copy-start.24 = (bf16[256,1024]{1,0:T(8,128)(2,1)S(1)}, bf16[256,1024]{1,0:T(8,128)(2,1)}, u32[]{:S(2)}) copy-start(bf16[256,1024]{1,0:T(8,128)(2,1)} %param.5) | copy-start | bytes 1572868
  38.4 52.0 %all-to-all-start = ((bf16[4,2,256,1024]{3,2,1,0:T(8,128)(2,1)}), bf16[4,2,256,1024]{3,2,1,0:T(8,128)(2,1)}, u32[]{:S(2)}, u32[]{:S(2)}) async-start(bf16[4,2,256,1024]{3,2,1,0:T(8,128)(2,1)} %broadcast_in_dim.111), calls=%async_computation | async-start | bytes 8388608 | tf_op jit(solution)/shard_map/all_to_all | solution.py:147
  43.5 4.5 %copy-start = (bf16[32,32,2048]{2,1,0:T(8,128)(2,1)S(1)}, bf16[32,32,2048]{2,1,0:T(8,128)(2,1)}, u32[]{:S(2)}) copy-start(bf16[32,32,2048]{2,1,0:T(8,128)(2,1)} %add_multiply_fusion) | copy-start | bytes 12582916
  116.6 1.2 copy-start.5
  117.8 5.3 %collective-permute-start.3 = (bf16[8,512]{1,0:T(8,128)(2,1)S(1)}, bf16[8,512]{1,0:T(8,128)(2,1)S(1)}, u32[]{:S(2)}, u32[]{:S(2)}) collective-permute-start(bf16[8,512]{1,0:T(8,128)(2,1)S(1)} %reshape.435), channel_id=1, source_target_pairs={{0,4},{4,8},{8,12},{12,16},{16,20},{20,24},{24,28},{28,32},{32,36}... | collective-permute-start | bytes 24584 | tf_op jit(solution)/shard_map/ppermute | solution.py:166
  125.8 15.2 %copy-start.4 = (f32[2048,256]{0,1:T(8,128)S(1)}, f32[2048,256]{0,1:T(8,128)}, u32[]{:S(2)}) copy-start(f32[2048,256]{0,1:T(8,128)} %fusion.67) | copy-start | bytes 6291460
  126.8 27.3 %all-to-all-start.1 = ((bf16[32,16,2,256]{3,1,2,0:T(8,128)(2,1)}), bf16[32,16,2,256]{3,1,2,0:T(8,128)(2,1)S(1)}, u32[]{:S(2)}, u32[]{:S(2)}) async-start(bf16[32,16,2,256]{3,1,2,0:T(8,128)(2,1)} %copy.28), calls=%async_computation.1 | async-start | bytes 1048576 | tf_op jit(solution)/shard_map/all_to_all | solution.py:181
  138.6 0.8 copy-start.2
  139.5 13.1 %collective-permute-start.2 = (bf16[1,512,256]{1,2,0:T(8,128)(2,1)S(1)}, bf16[1,512,256]{1,2,0:T(8,128)(2,1)}, u32[]{:S(2)}, u32[]{:S(2)}) collective-permute-start(bf16[1,512,256]{1,2,0:T(8,128)(2,1)S(1)} %constant_dynamic-slice_fusion.3), channel_id=1, source_target_pairs={{0,128},{128,0},{1,129},{129,1},{2,130},{130,2},{3,131},{131,3},{4... | collective-permute-start | bytes 786440 | tf_op jit(solution)/shard_map/ppermute | solution.py:161
  154.8 4.1 %copy-start.6 = (f32[16,1024]{1,0:T(8,128)S(1)}, f32[16,1024]{1,0:T(8,128)}, u32[]{:S(2)}) copy-start(f32[16,1024]{1,0:T(8,128)} %get-tuple-element.31) | copy-start | bytes 196612
  154.8 4.1 %copy-start.7 = (f32[16,1024]{1,0:T(8,128)S(1)}, f32[16,1024]{1,0:T(8,128)}, u32[]{:S(2)}) copy-start(f32[16,1024]{1,0:T(8,128)} %get-tuple-element.32) | copy-start | bytes 196612
  154.8 4.1 %copy-start.8 = (f32[16,1024]{1,0:T(8,128)S(1)}, f32[16,1024]{1,0:T(8,128)}, u32[]{:S(2)}) copy-start(f32[16,1024]{1,0:T(8,128)} %get-tuple-element.33) | copy-start | bytes 196612
  154.8 4.1 %copy-start.9 = (f32[16,1024]{1,0:T(8,128)S(1)}, f32[16,1024]{1,0:T(8,128)}, u32[]{:S(2)}) copy-start(f32[16,1024]{1,0:T(8,128)} %get-tuple-element.34) | copy-start | bytes 196612
  154.8 4.1 %copy-start.10 = (f32[16,1024]{1,0:T(8,128)S(1)}, f32[16,1024]{1,0:T(8,128)}, u32[]{:S(2)}) copy-start(f32[16,1024]{1,0:T(8,128)} %get-tuple-element.35) | copy-start | bytes 196612
  154.8 4.1 %copy-start.11 = (f32[16,1024]{1,0:T(8,128)S(1)}, f32[16,1024]{1,0:T(8,128)}, u32[]{:S(2)}) copy-start(f32[16,1024]{1,0:T(8,128)} %get-tuple-element.36) | copy-start | bytes 196612
  154.8 4.1 %copy-start.12 = (f32[16,1024]{1,0:T(8,128)S(1)}, f32[16,1024]{1,0:T(8,128)}, u32[]{:S(2)}) copy-start(f32[16,1024]{1,0:T(8,128)} %get-tuple-element.37) | copy-start | bytes 196612
  154.8 4.1 %copy-start.13 = (f32[16,1024]{1,0:T(8,128)S(1)}, f32[16,1024]{1,0:T(8,128)}, u32[]{:S(2)}) copy-start(f32[16,1024]{1,0:T(8,128)} %get-tuple-element.38) | copy-start | bytes 196612
  154.8 4.1 %copy-start.14 = (f32[16,1024]{1,0:T(8,128)S(1)}, f32[16,1024]{1,0:T(8,128)}, u32[]{:S(2)}) copy-start(f32[16,1024]{1,0:T(8,128)} %get-tuple-element.39) | copy-start | bytes 196612
  154.8 4.1 %copy-start.15 = (f32[16,1024]{1,0:T(8,128)S(1)}, f32[16,1024]{1,0:T(8,128)}, u32[]{:S(2)}) copy-start(f32[16,1024]{1,0:T(8,128)} %get-tuple-element.40) | copy-start | bytes 196612
  154.9 4.1 %copy-start.16 = (f32[16,1024]{1,0:T(8,128)S(1)}, f32[16,1024]{1,0:T(8,128)}, u32[]{:S(2)}) copy-start(f32[16,1024]{1,0:T(8,128)} %get-tuple-element.41) | copy-start | bytes 196612
  154.9 4.1 %copy-start.17 = (f32[16,1024]{1,0:T(8,128)S(1)}, f32[16,1024]{1,0:T(8,128)}, u32[]{:S(2)}) copy-start(f32[16,1024]{1,0:T(8,128)} %get-tuple-element.42) | copy-start | bytes 196612
  154.9 4.1 %copy-start.18 = (f32[16,1024]{1,0:T(8,128)S(1)}, f32[16,1024]{1,0:T(8,128)}, u32[]{:S(2)}) copy-start(f32[16,1024]{1,0:T(8,128)} %get-tuple-element.43) | copy-start | bytes 196612
  154.9 4.1 %copy-start.19 = (f32[16,1024]{1,0:T(8,128)S(1)}, f32[16,1024]{1,0:T(8,128)}, u32[]{:S(2)}) copy-start(f32[16,1024]{1,0:T(8,128)} %get-tuple-element.44) | copy-start | bytes 196612
  154.9 4.1 %copy-start.20 = (f32[16,1024]{1,0:T(8,128)S(1)}, f32[16,1024]{1,0:T(8,128)}, u32[]{:S(2)}) copy-start(f32[16,1024]{1,0:T(8,128)} %get-tuple-element.45) | copy-start | bytes 196612
  154.9 4.1 %copy-start.21 = (f32[16,1024]{1,0:T(8,128)S(1)}, f32[16,1024]{1,0:T(8,128)}, u32[]{:S(2)}) copy-start(f32[16,1024]{1,0:T(8,128)} %get-tuple-element.46) | copy-start | bytes 196612
  154.9 4.1 %copy-start.22 = (f32[16,1024]{1,0:T(8,128)S(1)}, f32[16,1024]{1,0:T(8,128)}, u32[]{:S(2)}) copy-start(f32[16,1024]{1,0:T(8,128)} %get-tuple-element.47) | copy-start | bytes 196612
  154.9 4.1 %copy-start.23 = (f32[16,1024]{1,0:T(8,128)S(1)}, f32[16,1024]{1,0:T(8,128)}, u32[]{:S(2)}) copy-start(f32[16,1024]{1,0:T(8,128)} %get-tuple-element.48) | copy-start | bytes 196612
  158.6 10.4 %slice-start = ((s8[8388608]{0:T(1024)(128)(4,1)}), s8[4194304]{0:T(1024)(128)(4,1)S(1)}, s32[]{:S(2)}) async-start(s8[8388608]{0:T(1024)(128)(4,1)} %bitcast.147), calls=%async_computation.4 | async-start | bytes 8388608
  159.0 9.9 %slice-start.1 = ((s8[8388608]{0:T(1024)(128)(4,1)}), s8[4194304]{0:T(1024)(128)(4,1)S(1)}, s32[]{:S(2)}) async-start(s8[8388608]{0:T(1024)(128)(4,1)} %bitcast.147), calls=%async_computation.5 | async-start | bytes 8388608
  171.4 0.7 copy-start.26
  171.6 10.0 %copy-start.25 = (f32[3,3,1024]{2,1,0:T(4,128)S(1)}, f32[3,3,1024]{2,1,0:T(4,128)}, u32[]{:S(2)}) copy-start(f32[3,3,1024]{2,1,0:T(4,128)} %param.7) | copy-start | bytes 110596
  171.9 9.7 %copy-start.3 = (bf16[1,512,512]{1,2,0:T(8,128)(2,1)S(1)}, bf16[1,512,512]{1,2,0:T(8,128)(2,1)}, u32[]{:S(2)}) copy-start(bf16[1,512,512]{1,2,0:T(8,128)(2,1)} %copy-done.2) | copy-start | bytes 1572868
  173.5 25.6 %all-to-all-start.2 = ((bf16[64,16,256]{2,1,0:T(8,128)(2,1)}), bf16[64,16,256]{2,1,0:T(8,128)(2,1)S(1)}, u32[]{:S(2)}, u32[]{:S(2)}) async-start(bf16[64,16,256]{2,1,0:T(8,128)(2,1)} %bitcast.61), calls=%async_computation.2 | async-start | bytes 1048576 | tf_op jit(solution)/shard_map/all_to_all | solution.py:191
  182.7 7.4 %collective-permute-start.4 = (bf16[1,1024,2]{1,2,0:T(2,128)(2,1)S(1)}, bf16[1,1024,2]{1,2,0:T(2,128)(2,1)S(1)}, u32[]{:S(2)}, u32[]{:S(2)}) collective-permute-start(bf16[1,1024,2]{1,2,0:T(2,128)(2,1)S(1)} %fusion.60), channel_id=1, source_target_pairs={{0,4},{4,8},{8,12},{12,16},{16,20},{20,24},{24,28},{28,32},{32,36}... | collective-permute-start | bytes 12296 | tf_op jit(solution)/shard_map/ppermute | solution.py:15
Sparse Core Ops, SparseCore 0:
  16.8 84.7 all-gather.2
where the time goes:
time: 209 us; the launch traced here: 208 us
  waiting for transfers between devices  55.2 us (26%)
  other arithmetic  46.3 us (22%)
  starting transfers between devices  41.1 us (20%)
  local copies, waits for them, and re-layouts  29.6 us (14%)
  matrix products  21.4 us (10%)
  between operations  14.2 us (7%)
    all_to_all x1, waiting for transfers between devices, shards(): lax.all_to_all(copies, 'ch', split_axis=0, concat_axis=3, tiled=True)  27.3 us
    another operation x6, other arithmetic, run(): return lax.with_sharding_constraint(mapped(*args), out_sharding)  16.2 us
    dot_general x1, matrix products, shards(): jnp.einsum('pdc,ld->pcl', whole_weight, whole_tokens, preferred_element_t...  10.9 us
    all_to_all x1, starting transfers between devices, shards(): lax.all_to_all(outgoing12, 'cq', split_axis=0, concat_axis=0, tiled=True)  10.7 us
    ppermute x1, waiting for transfers between devices, shards(): received = lax.ppermute(other_part, 'yh', swap)  9.8 us
    all_to_all x1, waiting for transfers between devices, shards(): lax.all_to_all(outgoing, ctx, split_axis=0, concat_axis=0, tiled=True)  9.01 us
    concatenate x1, other arithmetic, spectral_tables(): jnp.concatenate([weights * cos_b, jnp.where(first_row, alt_t / period, -(...  8.5 us
    all_to_all x1, starting transfers between devices, shards(): lax.all_to_all(outgoing, ctx, split_axis=0, concat_axis=0, tiled=True)  8.09 us
  transfers between devices with their start and end apart: 9, of which 7 were waited for; matrix products, arithmetic and copies ran while one was open for 28% of the time, Pallas kernels for 0%

commit v1 on v0

--- a/solution.py
+++ b/solution.py
@@ -144,7 +144,19 @@
         partner_tokens = lax.ppermute(tokens, "yh", swap)
         token_pair = by_half(half, tokens, partner_tokens)
         copies = jnp.broadcast_to(token_pair[None], (n_ch,) + token_pair.shape)
-        pieces = lax.all_to_all(copies, "ch", split_axis=0, concat_axis=3, tiled=True)
+        ways, here = (lax.axis_size("ch"), lax.axis_index("ch"))
+        width_2 = copies.shape[0] // ways
+        dims = list(copies.shape)
+        dims[0] = width_2
+        height = dims[3]
+        dims[3] = height * ways
+        full = jnp.zeros(dims, copies.dtype)
+        for mask in range(ways):
+            part = lax.dynamic_slice_in_dim(copies, (here ^ mask) * width_2, width_2, axis=0)
+            if mask:
+                part = lax.ppermute(part, "ch", [(d, d ^ mask) for d in range(ways)])
+            full = lax.dynamic_update_slice_in_dim(full, part, (here ^ mask) * height, axis=3)
+        pieces = full
         whole_tokens = pieces.reshape(2 * local_tokens, n_ch * local_features)
         forward, inverse = spectral_tables(tile_extent)
         spec_k = filter_spectra(long_filter[0], forward, tile_extent)

time: 209 us -> 201 us (0.962)
  local copies, waits for them, and re-layouts: 29.6 us -> 18.1 us
  waiting for transfers between devices: 55.2 us -> 65.4 us
  starting transfers between devices: 41.1 us -> 36.9 us
    ppermute x0 -> x3, waiting for transfers between devices: none -> 31.8 us  [shards(): part = lax.ppermute(part, 'ch', [(d, d ^ mask) for d in range(ways)])]
    all_to_all x1 -> x0, waiting for transfers between devices: 27.3 us -> none  [shards(): lax.all_to_all(copies, 'ch', split_axis=0, concat_axis=3, tiled=True)]
    reshape x1 -> x0, local copies, waits for them, and re-layouts: 7.81 us -> none  [shards(): whole_tokens = pieces.reshape(2 * local_tokens, n_ch * local_features)]
    all_to_all x1 -> x0, local copies, waits for them, and re-layouts: 7.43 us -> none  [shards(): lax.all_to_all(copies, 'ch', split_axis=0, concat_axis=3, tiled=True)]
    all_gather x1, waiting for transfers between devices: 0.01 us -> 7.12 us  [shards(): gathered = lax.all_gather(rows_pair, 'cq', axis=2, tiled=False)]
    all_to_all x1 -> x0, starting transfers between devices: 5.06 us -> none  [shards(): lax.all_to_all(copies, 'ch', split_axis=0, concat_axis=3, tiled=True)]
    dynamic_update_slice x0 -> x3, local copies, waits for them, and re-layouts: none -> 4.52 us  [shards(): lax.dynamic_update_slice_in_dim(full, part, (here ^ mask) * height, axis=3)]
    ppermute x0 -> x3, starting transfers between devices: none -> 3.95 us  [shards(): part = lax.ppermute(part, 'ch', [(d, d ^ mask) for d in range(ways)])]
  transfers between devices with their start and end apart: 9 -> 11, of which waited for: 7 -> 10; matrix products, arithmetic and copies ran while one was open for 28% -> 21% of each run, Pallas kernels for 0% -> 0%
where the time goes in v1:
time: 201 us; the launch traced here: 200 us
  waiting for transfers between devices  65.4 us (33%)
  other arithmetic  45.2 us (22%)
  starting transfers between devices  36.9 us (18%)
  matrix products  20.4 us (10%)
  local copies, waits for them, and re-layouts  18.1 us (9%)
  between operations  14.1 us (7%)
    ppermute x3, waiting for transfers between devices, shards(): part = lax.ppermute(part, 'ch', [(d, d ^ mask) for d in range(ways)])  31.8 us
    another operation x6, other arithmetic, run(): return lax.with_sharding_constraint(mapped(*args), out_sharding)  16.2 us
    dot_general x1, matrix products, shards(): jnp.einsum('pdc,ld->pcl', whole_weight, whole_tokens, preferred_element_t...  11.7 us
    all_to_all x1, waiting for transfers between devices, shards(): lax.all_to_all(outgoing, ctx, split_axis=0, concat_axis=0, tiled=True)  9.01 us
    all_to_all x1, starting transfers between devices, shards(): lax.all_to_all(outgoing, ctx, split_axis=0, concat_axis=0, tiled=True)  8.8 us
    ppermute x1, waiting for transfers between devices, shards(): received = lax.ppermute(other_part, 'yh', swap)  8.67 us
    concatenate x1, other arithmetic, spectral_tables(): jnp.concatenate([weights * cos_b, jnp.where(first_row, alt_t / period, -(...  8.54 us
    all_to_all x1, starting transfers between devices, shards(): lax.all_to_all(outgoing12, 'cq', split_axis=0, concat_axis=0, tiled=True)  8.4 us
  transfers between devices with their start and end apart: 11, of which 10 were waited for; matrix products, arithmetic and copies ran while one was open for 21% of the time, Pallas kernels for 0%

profile of v1, /device:TPU:1, one launch (start us, length us, event | category | flops | bytes accessed | tf_op | source)
XLA Modules:
  0.0 200.1 jit_solution(15073103764078163453)
XLA Ops:
  6.5 0.9 constant_dynamic-slice_fusion.4
  7.5 3.8 %collective-permute-start = (bf16[3,64,512]{2,1,0:T(8,128)(2,1)S(1)}, bf16[3,64,512]{2,1,0:T(8,128)(2,1)S(1)}, u32[]{:S(2)}, u32[]{:S(2)}) collective-permute-start(bf16[3,64,512]{2,1,0:T(8,128)(2,1)S(1)} %constant_dynamic-slice_fusion.4), channel_id=1, source_target_pairs={{0,128},{128,0},{1,129},{129,1},{2,130},{130,2},{3,131},{131,3},{4... | collective-permute-start | bytes 589832 | tf_op jit(solution)/shard_map/ppermute | solution.py:140
  11.3 3.6 %collective-permute-done = bf16[3,64,512]{2,1,0:T(8,128)(2,1)S(1)} collective-permute-done((bf16[3,64,512]{2,1,0:T(8,128)(2,1)S(1)}, bf16[3,64,512]{2,1,0:T(8,128)(2,1)S(1)}, u32[]{:S(2)}, u32[]{:S(2)}) %collective-permute-start) | collective-permute-done | bytes 196640 | tf_op jit(solution)/shard_map/ppermute | solution.py:140
  14.9 1.0 select_bitcast_fusion.3
  16.7 3.8 %collective-permute-start.1 = (bf16[256,1024]{1,0:T(8,128)(2,1)}, bf16[256,1024]{1,0:T(8,128)(2,1)S(1)}, u32[]{:S(2)}, u32[]{:S(2)}) collective-permute-start(bf16[256,1024]{1,0:T(8,128)(2,1)} %param.5), channel_id=1, source_target_pairs={{0,128},{128,0},{1,129},{129,1},{2,130},{130,2},{3,131},{131,3},{4... | collective-permute-start | bytes 1572872 | tf_op jit(solution)/shard_map/ppermute | solution.py:144
  20.5 1.3 convert_element_type.115
  23.6 1.0 fusion.42
  26.6 2.6 %fusion.67 = f32[2048,256]{0,1:T(8,128)} fusion(bf16[256,1024]{1,0:T(8,128)(2,1)S(1)} %bitcast.163, bf16[1024,1024]{1,0:T(8,128)(2,1)S(1)} %fusion.6, bf16[1024,1024]{1,0:T(8,128)(2,1)S(1)} %bitcast.153), kind=kOutput, calls=%fused_computation.199 | convolution fusion | flops 1082130432 | bytes 6815744 | tf_op jit(solution)/shard_map/dot_general | solution.py:60
  29.2 1.1 fusion.45
  30.3 1.6 add_multiply_fusion
  31.9 1.3 multiply_subtract_fusion
  33.2 2.5 %fusion.3 = bf16[1024,2048]{1,0:T(8,128)(2,1)} fusion(f32[32,32,2048]{2,1,0:T(8,128)S(1)} %multiply_subtract_fusion, f32[1024]{0:T(1024)S(1)} %select_multiply_fusion.1), kind=kLoop, calls=%fused_computation.6 | loop fusion | flops 4194304 | bytes 12587008 | tf_op jit(solution)/shard_map/convert.4 | solution.py:233
  35.6 2.8 %fusion.2 = bf16[1024,2048]{1,0:T(8,128)(2,1)} fusion(bf16[32,32,2048]{2,1,0:T(8,128)(2,1)S(1)} %add_multiply_fusion, bf16[2048]{0:T(1024)(128)(2,1)S(1)} %select_multiply_fusion, pred[1024]{0:T(1024)(128)(4,1)S(1)} %iota_compare_fusion), kind=kLoop, calls=%fused_computation.4 | loop fusion | flops 2097152 | bytes 8393728 | tf_op jit(solution)/shard_map/convert.5 | solution.py:233
  38.5 1.1 maximum_bitcast_fusion
  39.6 1.2 collective-permute-start.2
  40.9 2.4 %pad_maximum_fusion.1 = bf16[1024,2048]{1,0:T(8,128)(2,1)} fusion(bf16[1024,1024]{1,0:T(8,128)(2,1)S(1)} %fusion.6, bf16[1024,1024]{1,0:T(8,128)(2,1)S(1)} %bitcast.154), kind=kLoop, calls=%fused_computation.39 | loop fusion | flops 8388608 | bytes 8388608 | tf_op jit(solution)/shard_map/concatenate | solution.py:38
  43.3 2.5 %collective-permute-start.3 = (bf16[1,2,256,1024]{3,2,1,0:T(8,128)(2,1)}, bf16[1,2,256,1024]{3,2,1,0:T(8,128)(2,1)S(1)}, u32[]{:S(2)}, u32[]{:S(2)}) collective-permute-start(bf16[1,2,256,1024]{3,2,1,0:T(8,128)(2,1)} %maximum_bitcast_fusion), channel_id=1, source_target_pairs={{0,2},{1,3},{2,0},{3,1},{4,6},{5,7},{6,4},{7,5},{8,10},{9,11},{10,... | collective-permute-start | bytes 3145736 | tf_op jit(solution)/shard_map/ppermute | solution.py:157
  46.1 8.5 %pad_maximum_fusion = bf16[2048,2048]{1,0:T(8,128)(2,1)} fusion(bf16[1024,2048]{1,0:T(8,128)(2,1)} %fusion.2, bf16[1024,2048]{1,0:T(8,128)(2,1)} %fusion.3), kind=kLoop, calls=%fused_computation | loop fusion | flops 16777216 | bytes 16777216 | tf_op jit(solution)/shard_map/concatenate | solution.py:45
  54.6 2.6 %broadcast_in_dim.114 = bf16[1,2,256,4096]{3,2,1,0:T(8,128)(2,1)} broadcast(bf16[]{:T(256)} %constant.104.clone.1), dimensions={} | broadcast | bytes 4194306 | tf_op jit(solution)/shard_map/broadcast_in_dim | solution.py:153
  57.2 1.1 constant_dynamic-update-slice_fusion.3
  58.3 4.6 %collective-permute-done.2 = bf16[1,2,256,1024]{3,2,1,0:T(8,128)(2,1)S(1)} collective-permute-done((bf16[1,2,256,1024]{3,2,1,0:T(8,128)(2,1)}, bf16[1,2,256,1024]{3,2,1,0:T(8,128)(2,1)S(1)}, u32[]{:S(2)}, u32[]{:S(2)}) %collective-permute-start.2) | collective-permute-done | bytes 1048608 | tf_op jit(solution)/shard_map/ppermute | solution.py:157
  62.9 1.1 constant_dynamic-update-slice_fusion.2
  63.9 23.5 %collective-permute-done.3 = bf16[1,2,256,1024]{3,2,1,0:T(8,128)(2,1)S(1)} collective-permute-done((bf16[1,2,256,1024]{3,2,1,0:T(8,128)(2,1)}, bf16[1,2,256,1024]{3,2,1,0:T(8,128)(2,1)S(1)}, u32[]{:S(2)}, u32[]{:S(2)}) %collective-permute-start.3) | collective-permute-done | bytes 1048608 | tf_op jit(solution)/shard_map/ppermute | solution.py:157
  87.5 1.1 constant_dynamic-update-slice_fusion.1
  88.6 3.6 %collective-permute-done.4 = bf16[1,2,256,1024]{3,2,1,0:T(8,128)(2,1)} collective-permute-done((bf16[1,2,256,1024]{3,2,1,0:T(8,128)(2,1)}, bf16[1,2,256,1024]{3,2,1,0:T(8,128)(2,1)}, u32[]{:S(2)}, u32[]{:S(2)}) %collective-permute-start.4) | collective-permute-done | bytes 1048608 | tf_op jit(solution)/shard_map/ppermute | solution.py:157
  92.2 2.3 %constant_dynamic-update-slice_fusion = bf16[1,2,256,4096]{3,2,1,0:T(8,128)(2,1)} fusion(bf16[1,2,256,4096]{3,2,1,0:T(8,128)(2,1)} %constant_dynamic-update-slice_fusion.1, bf16[1,2,256,1024]{3,2,1,0:T(8,128)(2,1)} %collective-permute-done.4, s32[]{:T(128)S(6)} %select_n.214), kind=kLoop, calls=%fused_computation.191 | loop fusion | bytes 2097156 | tf_op jit(solution)/shard_map/dynamic_update_slice | solution.py:158
  94.6 7.1 %all-gather.3.cloned.1.call-done = bf16[3,2,2048,512]{3,2,1,0:T(8,128)(2,1)} async-done(((bf16[3,2,64,512]{3,2,1,0:T(8,128)(2,1)}), bf16[3,2,2048,512]{3,2,1,0:T(8,128)(2,1)}) %all-gather.3.cloned.1.call-update) | async-done | bytes 12582928 | tf_op jit(solution)/shard_map/all_gather | solution.py:142
  101.7 11.7 %convolution_convert_fusion = bf16[3,512,512]{1,2,0:T(8,128)(2,1)} fusion(bf16[512,4096,1]{1,0,2:T(8,128)(2,1)} %bitcast.17, bf16[3,4096,512]{2,1,0:T(8,128)(2,1)} %bitcast.170), kind=kOutput, calls=%fused_computation.51 | convolution fusion | flops 6443237376 | bytes 18350080 | tf_op jit(solution)/shard_map/pdc,ld->pcl/dot_general | solution.py:166
  113.4 1.3 slice.382
  114.8 1.5 collective-permute-start.6
  118.1 1.7 fusion.7
  120.8 8.4 %all-to-all-start = ((bf16[32,16,2,256]{3,1,2,0:T(8,128)(2,1)}), bf16[32,16,2,256]{3,1,2,0:T(8,128)(2,1)S(1)}, u32[]{:S(2)}, u32[]{:S(2)}) async-start(bf16[32,16,2,256]{3,1,2,0:T(8,128)(2,1)} %copy.27), calls=%async_computation | async-start | bytes 1048576 | tf_op jit(solution)/shard_map/all_to_all | solution.py:193
  129.2 1.1 slice.381
  131.1 3.0 %collective-permute-start.5 = (bf16[1,512,256]{1,2,0:T(8,128)(2,1)S(1)}, bf16[1,512,256]{1,2,0:T(8,128)(2,1)}, u32[]{:S(2)}, u32[]{:S(2)}) collective-permute-start(bf16[1,512,256]{1,2,0:T(8,128)(2,1)S(1)} %constant_dynamic-slice_fusion.3), channel_id=1, source_target_pairs={{0,128},{128,0},{1,129},{129,1},{2,130},{130,2},{3,131},{131,3},{4... | collective-permute-start | bytes 786440 | tf_op jit(solution)/shard_map/ppermute | solution.py:173
  134.1 0.9 slice_bitcast_fusion.30
  135.8 8.7 %collective-permute-done.5 = bf16[1,512,256]{1,2,0:T(8,128)(2,1)} collective-permute-done((bf16[1,512,256]{1,2,0:T(8,128)(2,1)S(1)}, bf16[1,512,256]{1,2,0:T(8,128)(2,1)}, u32[]{:S(2)}, u32[]{:S(2)}) %collective-permute-start.5) | collective-permute-done | bytes 262176 | tf_op jit(solution)/shard_map/ppermute | solution.py:173
  144.5 1.3 all-to-all-done
  146.6 3.6 %fusion.4 = f32[16,16,2048]{2,1,0:T(8,128)S(1)} fusion(bf16[16,16,1024]{2,1,0:T(8,128)(2,1)S(1)} %dot_general.19, bf16[1024,2048]{1,0:T(8,128)(2,1)} %pad_maximum_fusion.1), kind=kOutput, calls=%fused_computation.40 | convolution fusion | flops 1073741824 | bytes 6815744 | tf_op jit(solution)/shard_map/dot_general | solution.py:69
  150.6 4.5 %subtract_convert_fusion.1 = bf16[16,16,1024]{2,1,0:T(8,128)(2,1)S(1)} fusion(f32[16,16,1024]{2,1,0:T(8,128)S(1)} %get-tuple-element.50, f32[16,1024]{1,0:T(8,128)S(1)} %copy-done.6, f32[16,1024]{1,0:T(8,128)S(1)} %copy-done.7, f32[16,1024]{1,0:T(8,128)S(1)} %copy-done.9, f32[16,1024]{1,0:T(8,128)S(1)} %copy-done.10, f32[16,1024]{1,0:T(8,128)S(1)} %copy-done.11, ...), kind=kLoop, calls=%fused_computation.75 | loop fusion | flops 17039360 | bytes 4719616 | tf_op jit(solution)/shard_map/convert.2 | solution.py:233
  155.2 5.2 %select_convert_fusion = bf16[16,16,1024]{2,1,0:T(8,128)(2,1)S(1)} fusion(f32[16,16,1024]{2,1,0:T(8,128)S(1)} %get-tuple-element.50, f32[16,16,1024]{2,1,0:T(8,128)S(1)} %get-tuple-element.49, f32[16,1024]{1,0:T(8,128)S(1)} %get-tuple-element.18, f32[16,1024]{1,0:T(8,128)S(1)} %get-tuple-element.19, f32[16,1024]{1,0:T(8,128)S(1)} %get-tuple-element.20, ...), kind=kLoop, calls=%fused_computation.74 | loop fusion | flops 25165824 | bytes 4719616 | tf_op jit(solution)/shard_map/convert.3 | solution.py:233
  160.6 2.4 %fusion = f32[16,16,2048]{2,1,0:T(8,128)S(1)} fusion(bf16[2048,2048]{1,0:T(8,128)(2,1)S(1)} %bitcast.152, bf16[16,16,1024]{2,1,0:T(8,128)(2,1)S(1)} %select_convert_fusion, bf16[16,16,1024]{2,1,0:T(8,128)(2,1)S(1)} %subtract_convert_fusion.1), kind=kOutput, calls=%fused_computation.1 | convolution fusion | flops 2149580800 | bytes 11534336 | tf_op jit(solution)/shard_map/dot_general | solution.py:90
  163.7 1.4 fusion.22
  165.2 8.8 %all-to-all-start.1 = ((bf16[64,16,256]{2,1,0:T(8,128)(2,1)}), bf16[64,16,256]{2,1,0:T(8,128)(2,1)S(1)}, u32[]{:S(2)}, u32[]{:S(2)}) async-start(bf16[64,16,256]{2,1,0:T(8,128)(2,1)} %bitcast.62), calls=%async_computation.1 | async-start | bytes 1048576 | tf_op jit(solution)/shard_map/all_to_all | solution.py:203
  174.0 1.0 broadcast_select_fusion
  175.1 3.5 %collective-permute-start.7 = (bf16[1,1024,2]{1,2,0:T(2,128)(2,1)S(1)}, bf16[1,1024,2]{1,2,0:T(2,128)(2,1)S(1)}, u32[]{:S(2)}, u32[]{:S(2)}) collective-permute-start(bf16[1,1024,2]{1,2,0:T(2,128)(2,1)S(1)} %fusion.60), channel_id=1, source_target_pairs={{0,4},{4,8},{8,12},{12,16},{16,20},{20,24},{24,28},{28,32},{32,36}... | collective-permute-start | bytes 12296 | tf_op jit(solution)/shard_map/ppermute | solution.py:15
  178.7 3.7 %collective-permute-done.7 = bf16[1,1024,2]{1,2,0:T(2,128)(2,1)S(1)} collective-permute-done((bf16[1,1024,2]{1,2,0:T(2,128)(2,1)S(1)}, bf16[1,1024,2]{1,2,0:T(2,128)(2,1)S(1)}, u32[]{:S(2)}, u32[]{:S(2)}) %collective-permute-start.7) | collective-permute-done | bytes 4128 | tf_op jit(solution)/shard_map/ppermute | solution.py:15
  182.4 9.0 %all-to-all-done.1 = bf16[64,16,256]{2,1,0:T(8,128)(2,1)S(1)} async-done(((bf16[64,16,256]{2,1,0:T(8,128)(2,1)}), bf16[64,16,256]{2,1,0:T(8,128)(2,1)S(1)}, u32[]{:S(2)}, u32[]{:S(2)}) %all-to-all-start.1) | async-done | bytes 524320 | tf_op jit(solution)/shard_map/all_to_all | solution.py:203
  192.3 1.0 copy.32
  (104 shorter events, 12.1 us)
Async XLA Ops:
  6.5 95.1 %all-gather.3.cloned.1.call-start = ((), (), s32[]{:S(2)}) async-start(), calls=%async_computation.2 | async-start | bytes 12976128 | tf_op jit(solution)/shard_map/all_gather | solution.py:142
  7.5 7.4 %collective-permute-start = (bf16[3,64,512]{2,1,0:T(8,128)(2,1)S(1)}, bf16[3,64,512]{2,1,0:T(8,128)(2,1)S(1)}, u32[]{:S(2)}, u32[]{:S(2)}) collective-permute-start(bf16[3,64,512]{2,1,0:T(8,128)(2,1)S(1)} %constant_dynamic-slice_fusion.4), channel_id=1, source_target_pairs={{0,128},{128,0},{1,129},{129,1},{2,130},{130,2},{3,131},{131,3},{4... | collective-permute-start | bytes 589832 | tf_op jit(solution)/shard_map/ppermute | solution.py:140
  16.7 21.8 %collective-permute-start.1 = (bf16[256,1024]{1,0:T(8,128)(2,1)}, bf16[256,1024]{1,0:T(8,128)(2,1)S(1)}, u32[]{:S(2)}, u32[]{:S(2)}) collective-permute-start(bf16[256,1024]{1,0:T(8,128)(2,1)} %param.5), channel_id=1, source_target_pairs={{0,128},{128,0},{1,129},{129,1},{2,130},{130,2},{3,131},{131,3},{4... | collective-permute-start | bytes 1572872 | tf_op jit(solution)/shard_map/ppermute | solution.py:144
  35.6 2.8 %copy-start.21 = (bf16[256,1024]{1,0:T(8,128)(2,1)S(1)}, bf16[256,1024]{1,0:T(8,128)(2,1)}, u32[]{:S(2)}) copy-start(bf16[256,1024]{1,0:T(8,128)(2,1)} %param.5) | copy-start | bytes 1572868
  39.6 6.1 %slice-start.2 = ((f32[3,3,1024]{2,1,0:T(4,128)}), f32[2,3,1024]{2,1,0:T(4,128)S(1)}, s32[]{:S(2)}) async-start(f32[3,3,1024]{2,1,0:T(4,128)} %param.7), calls=%async_computation.5 | async-start | bytes 65536 | tf_op jit(solution)/shard_map/slice | solution.py:181
  39.6 23.2 %collective-permute-start.2 = (bf16[1,2,256,1024]{3,2,1,0:T(8,128)(2,1)}, bf16[1,2,256,1024]{3,2,1,0:T(8,128)(2,1)S(1)}, u32[]{:S(2)}, u32[]{:S(2)}) collective-permute-start(bf16[1,2,256,1024]{3,2,1,0:T(8,128)(2,1)} %maximum_bitcast_fusion), channel_id=1, source_target_pairs={{0,1},{1,0},{2,3},{3,2},{4,5},{5,4},{6,7},{7,6},{8,9},{9,8},{10,11... | collective-permute-start | bytes 3145736 | tf_op jit(solution)/shard_map/ppermute | solution.py:157
  43.3 44.2 %collective-permute-start.3 = (bf16[1,2,256,1024]{3,2,1,0:T(8,128)(2,1)}, bf16[1,2,256,1024]{3,2,1,0:T(8,128)(2,1)S(1)}, u32[]{:S(2)}, u32[]{:S(2)}) collective-permute-start(bf16[1,2,256,1024]{3,2,1,0:T(8,128)(2,1)} %maximum_bitcast_fusion), channel_id=1, source_target_pairs={{0,2},{1,3},{2,0},{3,1},{4,6},{5,7},{6,4},{7,5},{8,10},{9,11},{10,... | collective-permute-start | bytes 3145736 | tf_op jit(solution)/shard_map/ppermute | solution.py:157
  45.8 46.4 %collective-permute-start.4 = (bf16[1,2,256,1024]{3,2,1,0:T(8,128)(2,1)}, bf16[1,2,256,1024]{3,2,1,0:T(8,128)(2,1)}, u32[]{:S(2)}, u32[]{:S(2)}) collective-permute-start(bf16[1,2,256,1024]{3,2,1,0:T(8,128)(2,1)} %maximum_bitcast_fusion), channel_id=1, source_target_pairs={{0,3},{1,2},{2,1},{3,0},{4,7},{5,6},{6,5},{7,4},{8,11},{9,10},{10,... | collective-permute-start | bytes 3145736 | tf_op jit(solution)/shard_map/ppermute | solution.py:157
  114.8 2.3 %collective-permute-start.6 = (bf16[8,512]{1,0:T(8,128)(2,1)S(1)}, bf16[8,512]{1,0:T(8,128)(2,1)S(1)}, u32[]{:S(2)}, u32[]{:S(2)}) collective-permute-start(bf16[8,512]{1,0:T(8,128)(2,1)S(1)} %reshape.438), channel_id=1, source_target_pairs={{0,4},{4,8},{8,12},{12,16},{16,20},{20,24},{24,28},{28,32},{32,36}... | collective-permute-start | bytes 24584 | tf_op jit(solution)/shard_map/ppermute | solution.py:178
  119.8 14.3 %copy-start.2 = (f32[2048,256]{0,1:T(8,128)S(1)}, f32[2048,256]{0,1:T(8,128)}, u32[]{:S(2)}) copy-start(f32[2048,256]{0,1:T(8,128)} %fusion.67) | copy-start | bytes 6291460
  120.8 25.0 %all-to-all-start = ((bf16[32,16,2,256]{3,1,2,0:T(8,128)(2,1)}), bf16[32,16,2,256]{3,1,2,0:T(8,128)(2,1)S(1)}, u32[]{:S(2)}, u32[]{:S(2)}) async-start(bf16[32,16,2,256]{3,1,2,0:T(8,128)(2,1)} %copy.27), calls=%async_computation | async-start | bytes 1048576 | tf_op jit(solution)/shard_map/all_to_all | solution.py:193
  130.3 0.8 copy-start
  131.1 13.4 %collective-permute-start.5 = (bf16[1,512,256]{1,2,0:T(8,128)(2,1)S(1)}, bf16[1,512,256]{1,2,0:T(8,128)(2,1)}, u32[]{:S(2)}, u32[]{:S(2)}) collective-permute-start(bf16[1,512,256]{1,2,0:T(8,128)(2,1)S(1)} %constant_dynamic-slice_fusion.3), channel_id=1, source_target_pairs={{0,128},{128,0},{1,129},{129,1},{2,130},{130,2},{3,131},{131,3},{4... | collective-permute-start | bytes 786440 | tf_op jit(solution)/shard_map/ppermute | solution.py:173
  146.4 4.1 %copy-start.3 = (f32[16,1024]{1,0:T(8,128)S(1)}, f32[16,1024]{1,0:T(8,128)}, u32[]{:S(2)}) copy-start(f32[16,1024]{1,0:T(8,128)} %get-tuple-element.31) | copy-start | bytes 196612
  146.4 4.1 %copy-start.4 = (f32[16,1024]{1,0:T(8,128)S(1)}, f32[16,1024]{1,0:T(8,128)}, u32[]{:S(2)}) copy-start(f32[16,1024]{1,0:T(8,128)} %get-tuple-element.32) | copy-start | bytes 196612
  146.4 4.1 %copy-start.5 = (f32[16,1024]{1,0:T(8,128)S(1)}, f32[16,1024]{1,0:T(8,128)}, u32[]{:S(2)}) copy-start(f32[16,1024]{1,0:T(8,128)} %get-tuple-element.33) | copy-start | bytes 196612
  146.4 4.1 %copy-start.6 = (f32[16,1024]{1,0:T(8,128)S(1)}, f32[16,1024]{1,0:T(8,128)}, u32[]{:S(2)}) copy-start(f32[16,1024]{1,0:T(8,128)} %get-tuple-element.34) | copy-start | bytes 196612
  146.4 4.1 %copy-start.7 = (f32[16,1024]{1,0:T(8,128)S(1)}, f32[16,1024]{1,0:T(8,128)}, u32[]{:S(2)}) copy-start(f32[16,1024]{1,0:T(8,128)} %get-tuple-element.35) | copy-start | bytes 196612
  146.4 4.1 %copy-start.8 = (f32[16,1024]{1,0:T(8,128)S(1)}, f32[16,1024]{1,0:T(8,128)}, u32[]{:S(2)}) copy-start(f32[16,1024]{1,0:T(8,128)} %get-tuple-element.36) | copy-start | bytes 196612
  146.5 4.1 %copy-start.9 = (f32[16,1024]{1,0:T(8,128)S(1)}, f32[16,1024]{1,0:T(8,128)}, u32[]{:S(2)}) copy-start(f32[16,1024]{1,0:T(8,128)} %get-tuple-element.37) | copy-start | bytes 196612
  146.5 4.1 %copy-start.10 = (f32[16,1024]{1,0:T(8,128)S(1)}, f32[16,1024]{1,0:T(8,128)}, u32[]{:S(2)}) copy-start(f32[16,1024]{1,0:T(8,128)} %get-tuple-element.38) | copy-start | bytes 196612
  146.5 4.1 %copy-start.11 = (f32[16,1024]{1,0:T(8,128)S(1)}, f32[16,1024]{1,0:T(8,128)}, u32[]{:S(2)}) copy-start(f32[16,1024]{1,0:T(8,128)} %get-tuple-element.39) | copy-start | bytes 196612
  146.5 4.1 %copy-start.12 = (f32[16,1024]{1,0:T(8,128)S(1)}, f32[16,1024]{1,0:T(8,128)}, u32[]{:S(2)}) copy-start(f32[16,1024]{1,0:T(8,128)} %get-tuple-element.40) | copy-start | bytes 196612
  146.5 4.1 %copy-start.13 = (f32[16,1024]{1,0:T(8,128)S(1)}, f32[16,1024]{1,0:T(8,128)}, u32[]{:S(2)}) copy-start(f32[16,1024]{1,0:T(8,128)} %get-tuple-element.41) | copy-start | bytes 196612
  146.5 4.1 %copy-start.14 = (f32[16,1024]{1,0:T(8,128)S(1)}, f32[16,1024]{1,0:T(8,128)}, u32[]{:S(2)}) copy-start(f32[16,1024]{1,0:T(8,128)} %get-tuple-element.42) | copy-start | bytes 196612
  146.5 4.1 %copy-start.15 = (f32[16,1024]{1,0:T(8,128)S(1)}, f32[16,1024]{1,0:T(8,128)}, u32[]{:S(2)}) copy-start(f32[16,1024]{1,0:T(8,128)} %get-tuple-element.43) | copy-start | bytes 196612
  146.5 4.1 %copy-start.16 = (f32[16,1024]{1,0:T(8,128)S(1)}, f32[16,1024]{1,0:T(8,128)}, u32[]{:S(2)}) copy-start(f32[16,1024]{1,0:T(8,128)} %get-tuple-element.44) | copy-start | bytes 196612
  146.5 4.1 %copy-start.17 = (f32[16,1024]{1,0:T(8,128)S(1)}, f32[16,1024]{1,0:T(8,128)}, u32[]{:S(2)}) copy-start(f32[16,1024]{1,0:T(8,128)} %get-tuple-element.45) | copy-start | bytes 196612
  146.5 4.1 %copy-start.18 = (f32[16,1024]{1,0:T(8,128)S(1)}, f32[16,1024]{1,0:T(8,128)}, u32[]{:S(2)}) copy-start(f32[16,1024]{1,0:T(8,128)} %get-tuple-element.46) | copy-start | bytes 196612
  146.6 4.1 %copy-start.19 = (f32[16,1024]{1,0:T(8,128)S(1)}, f32[16,1024]{1,0:T(8,128)}, u32[]{:S(2)}) copy-start(f32[16,1024]{1,0:T(8,128)} %get-tuple-element.47) | copy-start | bytes 196612
  146.6 4.1 %copy-start.20 = (f32[16,1024]{1,0:T(8,128)S(1)}, f32[16,1024]{1,0:T(8,128)}, u32[]{:S(2)}) copy-start(f32[16,1024]{1,0:T(8,128)} %get-tuple-element.48) | copy-start | bytes 196612
  150.2 10.4 %slice-start = ((s8[8388608]{0:T(1024)(128)(4,1)}), s8[4194304]{0:T(1024)(128)(4,1)S(1)}, s32[]{:S(2)}) async-start(s8[8388608]{0:T(1024)(128)(4,1)} %bitcast.151), calls=%async_computation.3 | async-start | bytes 8388608
  150.6 9.9 %slice-start.1 = ((s8[8388608]{0:T(1024)(128)(4,1)}), s8[4194304]{0:T(1024)(128)(4,1)S(1)}, s32[]{:S(2)}) async-start(s8[8388608]{0:T(1024)(128)(4,1)} %bitcast.151), calls=%async_computation.4 | async-start | bytes 8388608
  163.1 0.7 copy-start.23
  163.3 10.7 %copy-start.22 = (f32[3,3,1024]{2,1,0:T(4,128)S(1)}, f32[3,3,1024]{2,1,0:T(4,128)}, u32[]{:S(2)}) copy-start(f32[3,3,1024]{2,1,0:T(4,128)} %param.7) | copy-start | bytes 110596
  163.6 10.4 %copy-start.1 = (bf16[1,512,512]{1,2,0:T(8,128)(2,1)S(1)}, bf16[1,512,512]{1,2,0:T(8,128)(2,1)}, u32[]{:S(2)}) copy-start(bf16[1,512,512]{1,2,0:T(8,128)(2,1)} %copy-done) | copy-start | bytes 1572868
  165.2 26.3 %all-to-all-start.1 = ((bf16[64,16,256]{2,1,0:T(8,128)(2,1)}), bf16[64,16,256]{2,1,0:T(8,128)(2,1)S(1)}, u32[]{:S(2)}, u32[]{:S(2)}) async-start(bf16[64,16,256]{2,1,0:T(8,128)(2,1)} %bitcast.62), calls=%async_computation.1 | async-start | bytes 1048576 | tf_op jit(solution)/shard_map/all_to_all | solution.py:203
  175.1 7.4 %collective-permute-start.7 = (bf16[1,1024,2]{1,2,0:T(2,128)(2,1)S(1)}, bf16[1,1024,2]{1,2,0:T(2,128)(2,1)S(1)}, u32[]{:S(2)}, u32[]{:S(2)}) collective-permute-start(bf16[1,1024,2]{1,2,0:T(2,128)(2,1)S(1)} %fusion.60), channel_id=1, source_target_pairs={{0,4},{4,8},{8,12},{12,16},{16,20},{20,24},{24,28},{28,32},{32,36}... | collective-permute-start | bytes 12296 | tf_op jit(solution)/shard_map/ppermute | solution.py:15
Sparse Core Ops, SparseCore 0:
  16.8 84.8 all-gather.2
